TPU v7x, 512 devices: a whole 4x8x8 slice. The times are simulated.
512 devices in a mesh: ta: 32 (over y, x), pb: 16 (over z, core).
Axes of the slice: x: 4, y: 8, z: 8, core: 2. Of those that a mesh axis runs over, the one named last changes fastest.
Arguments:
- particles: float32 [2, 2097152], P(None, ('ta', 'pb')), may hold values from -6 to 6
- weights: bfloat16 [2097152], P(('ta', 'pb')), may hold values from 0.5 to 2
- cell_index: int32 [2097152], P(('ta', 'pb')), may hold values from 0 to 9215
- target_group: int32 [2097152, 1], P(('ta', 'pb')), may hold values from 0 to 31; in each aligned block of 4096 rows (0 to 4095, 4096 to 8191, ...) at most 256 rows name the same one
- target_slice: int32 [2097152], P(('ta', 'pb')), may hold values from 0 to 3
- laser_x: float32 [96], replicated, may hold values from 0.3 to 1.5
- laser_y: float32 [96], replicated, may hold values from 0.3 to 1.5
- mode_x: float32 [96], replicated, may hold values from 0.3 to 1.5
- mode_y: float32 [96], replicated, may hold values from 0.3 to 1.5
- along_coeff: float32 [96, 96], replicated, may hold values from 0.2 to 2
- across_coeff: float32 [96, 96], replicated, may hold values from 0.1 to 1
Outputs:
- arrivals: float32 [2, 4194304], P(None, ('ta', 'pb'))
- radiation: float32 [2, 128], P(None, 'ta')
Inputs may be any that keep to these rules, and one draw needn't show every extreme that they name: `target_group`: in the rows of one device at most 256 rows name the same group, and in every draw some group is named by exactly 256 rows of some device.
All inputs are finite; a program needn't handle non-finite values.
Results may differ from a plain program's by a relative error of at most 0.0009.
Values sent between devices are 32-bit elements; how exact they have to be, the bound alone decides.
No kernel may reach another device: no remote copies, remote signals or barrier semaphores. Data moves between devices by JAX's collectives and lax.ppermute only.
A program may use at most 64 MiB of HBM per device.

v0:
```python
import math
import jax
import jax.numpy as jnp
from jax import lax
from jax.sharding import PartitionSpec as P

SL_DEV = 4
PS_DEV = 1024
HARM = 48
PERIODS = 2
DISPERSION = 3.0
LASER_GAIN = 1.0
KICK_GAIN = 0.5
SLIP_GAIN = 0.05


def with_halo(x, sides, width):
    for axis, dim in sides:
        peers, length = (lax.axis_size(axis), x.shape[dim])
        up = [(i, (i + 1) % peers) for i in range(peers - 1)]
        down = [(j, i) for i, j in up]
        last = lax.slice_in_dim(x, length - width, length, axis=dim)
        leading = lax.slice_in_dim(x, 0, width, axis=dim)
        before = lax.ppermute(last, axis, up)
        after = lax.ppermute(leading, axis, down)
        x = jnp.concatenate([before, x, after], axis=dim)
    return x


def shifted(value, axis, steps):
    count = lax.axis_size(axis)
    leading, last = (max(0, -steps), min(count, count - steps))
    return lax.ppermute(value, axis, [(source, source + steps) for source in range(leading, last)])


def lookup(values_table, positions):
    matches = positions[None, :] == jnp.arange(values_table.shape[0], dtype=jnp.int32)[:, None]
    return jnp.sum(jnp.where(matches, values_table[:, None], 0.0), axis=0)


def arrival_slots(destination, groups):
    count = destination.shape[0]
    block_size = math.gcd(count, 512)
    turn_count = count // block_size
    onehot = (destination[:, None] == jnp.arange(groups, dtype=jnp.int32)[None, :]).astype(
        jnp.bfloat16
    )
    onehot = onehot.reshape(turn_count, block_size, groups)
    earlier = (jnp.arange(block_size)[:, None] > jnp.arange(block_size)[None, :]).astype(
        jnp.bfloat16
    )

    def count_step(counted, onehot_rows):
        before = (
            jnp.dot(earlier, onehot_rows, preferred_element_type=jnp.float32) + counted[None, :]
        )
        rows_f = onehot_rows.astype(jnp.float32)
        return (counted + jnp.sum(rows_f, axis=0), jnp.sum(before * rows_f, axis=1))

    _, arrival = lax.scan(count_step, jnp.zeros((groups,), jnp.float32), onehot)
    return arrival.reshape(count).astype(jnp.int32)


def deposit(arrived_weight, got_slice, got_cell, slice_count, grid_x, grid_y):
    slot_count = arrived_weight.shape[0]
    block_size = math.gcd(slot_count, 2048)
    turn_count = slot_count // block_size
    block_items = (
        arrived_weight.reshape(turn_count, block_size),
        got_slice.reshape(turn_count, block_size),
        got_cell.reshape(turn_count, block_size),
    )

    def deposit_step(running, items):
        block_weight, block_slice, block_cell = items
        on_slice = block_slice[None, :] == jnp.arange(slice_count, dtype=jnp.int32)[:, None]
        on_row = (block_cell // grid_y)[None, :] == jnp.arange(grid_x, dtype=jnp.int32)[:, None]
        left = jnp.where(
            on_slice[:, None, :] & on_row[None, :, :],
            block_weight[None, None, :],
            jnp.zeros((), jnp.bfloat16),
        )
        left = left.reshape(slice_count * grid_x, block_size)
        right = (
            (block_cell % grid_y)[:, None] == jnp.arange(grid_y, dtype=jnp.int32)[None, :]
        ).astype(jnp.bfloat16)
        return (running + jnp.dot(left, right, preferred_element_type=jnp.float32), None)

    running, _ = lax.scan(
        deposit_step, jnp.zeros((slice_count * grid_x, grid_y), jnp.float32), block_items
    )
    return running.reshape(slice_count, grid_x * grid_y)


def stencil(extended, sideways, coeff_long, coeff_cross, grid_y):
    centre = sideways[:, grid_y:-grid_y]
    along_diff = extended[2:] - extended[:-2]
    across = sideways[:, 2 * grid_y :] + sideways[:, : -2 * grid_y]
    column = jnp.arange(centre.shape[1], dtype=jnp.int32) % grid_y
    upper_y = jnp.where(column < grid_y - 1, jnp.pad(centre, ((0, 0), (0, 1)))[:, 1:], 0.0)
    lower_y = jnp.where(column > 0, jnp.pad(centre, ((0, 0), (1, 0)))[:, :-1], 0.0)
    return coeff_long[None, :] * along_diff + coeff_cross[None, :] * (
        4.0 * centre - across - upper_y - lower_y
    )


def body(
    particles,
    weights,
    cell_index,
    target_group,
    target_slice,
    laser_x,
    laser_y,
    mode_x,
    mode_y,
    along_coeff,
    across_coeff,
):
    groups = lax.axis_size("ta")
    splits = lax.axis_size("pb")
    grid_x = laser_x.shape[0]
    grid_y = laser_y.shape[0]
    cell_count = grid_x * grid_y
    per_device = particles.shape[1]
    capacity = 2 * per_device // groups
    slot_count = groups * capacity
    row_x = cell_index // grid_y
    row_y = cell_index % grid_y
    energy = particles[1] + LASER_GAIN * lookup(laser_x, row_x) * lookup(laser_y, row_y) * jnp.sin(
        particles[0]
    )
    phases = particles[0] + DISPERSION * energy
    destination = target_group[:, 0]
    position = destination * capacity + arrival_slots(destination, groups)
    send_float = (
        jnp.zeros((3, slot_count), jnp.float32)
        .at[:, position]
        .set(jnp.stack([phases, energy, weights.astype(jnp.float32)]))
    )
    send_index = (
        jnp.zeros((1, slot_count), jnp.int32)
        .at[0, position]
        .set(target_slice * cell_count + cell_index)
    )
    got_float, got_index = (
        lax.all_to_all(
            send_float.reshape(3, groups, capacity), "ta", split_axis=1, concat_axis=1, tiled=True
        ),
        lax.all_to_all(
            send_index.reshape(1, groups, capacity), "ta", split_axis=1, concat_axis=1, tiled=True
        ),
    )
    got_float = got_float.reshape(3, slot_count)
    combined = got_index.reshape(slot_count)
    arrived_weight = got_float[2]
    got_slice = combined // cell_count
    got_cell = combined % cell_count
    partial_value = deposit(
        arrived_weight.astype(jnp.bfloat16), got_slice, got_cell, SL_DEV, grid_x, grid_y
    )
    long_flat = along_coeff.reshape(cell_count)
    cross_flat = across_coeff.reshape(cell_count)
    summed = lax.psum(partial_value, "pb")
    extended = with_halo(summed, (("ta", 0),), 1)
    sideways = jnp.pad(extended[1:-1], ((0, 0), (grid_y, grid_y)))
    force_map = stencil(extended, sideways, long_flat, cross_flat, grid_y)
    kicked = got_float[1] + jnp.take(force_map.reshape(-1), combined)
    got_phase = got_float[0]
    profile = lookup(mode_x, got_cell // grid_y) * lookup(mode_y, got_cell % grid_y)
    weighted = arrived_weight * profile
    select = (got_slice[None, :] == jnp.arange(SL_DEV, dtype=jnp.int32)[:, None]).astype(
        jnp.float32
    )
    couple = 1.0 / math.sqrt(splits * PS_DEV)
    radiation = jnp.zeros((2, SL_DEV), jnp.float32)
    for period in range(PERIODS):
        harmonic_phase = HARM * got_phase
        cosine = jnp.cos(harmonic_phase)
        sine_part = jnp.sin(harmonic_phase)
        local_sums = jnp.stack(
            [
                jnp.sum(select * (weighted * cosine)[None, :], axis=1),
                jnp.sum(select * (-weighted * sine_part)[None, :], axis=1),
            ]
        )
        bunching = lax.psum(local_sums, "pb")
        radiation = radiation + couple * bunching
        real_here = jnp.sum(select * radiation[0][:, None], axis=0)
        imag_here = jnp.sum(select * radiation[1][:, None], axis=0)
        kicked = kicked + KICK_GAIN * profile * (real_here * cosine - imag_here * sine_part)
        got_phase = got_phase + SLIP_GAIN * kicked
        incoming = shifted(radiation[:, -1:], "ta", 1)
        radiation = jnp.concatenate([incoming, radiation[:, :-1]], axis=1)
    filled = arrived_weight > 0
    result = jnp.stack([jnp.where(filled, got_phase, 0.0), jnp.where(filled, kicked, 0.0)])
    return (result, radiation)


def solution(mesh):
    return jax.shard_map(
        body,
        mesh=mesh,
        in_specs=(
            P(None, ("ta", "pb")),
            P(("ta", "pb")),
            P(("ta", "pb")),
            P(("ta", "pb"), None),
            P(("ta", "pb")),
            P(),
            P(),
            P(),
            P(),
            P(),
            P(),
        ),
        out_specs=(P(None, ("ta", "pb")), P(None, "ta")),
        check_vma=False,
    )
```

profile of v0, /device:TPU:32, one launch (start us, length us, event | category | flops | bytes accessed | tf_op | source)
XLA Modules:
  0.0 320.8 jit_solution(3291533808186617567)
XLA Ops:
  7.8 1.4 reduce.17
  9.3 4.0 %while.26 = (s32[]{:T(128)}, f32[32]{0:T(128)S(1)}, f32[8,512]{1,0:T(8,128)S(1)}, bf16[8,512,32]{1,2,0:T(8,128)(2,1)S(1)}, s32[]{:T(128)}, /*index=5*/s32[]{:T(128)}) while((s32[]{:T(128)}, f32[32]{0:T(128)S(1)}, f32[8,512]{1,0:T(8,128)S(1)}, bf16[8,512,32]{1,2,0:T(8,128)(2,1)S(1)}, s32[]{:T(128)}, /*index=5*/s32[]{:T(128)}) %tuple.81), condition=%wide.region_3.4_spmd.clone, body=%wide.region_0.3_spmd.clone.sunk | while | flops 17399332 | bytes 106719 | solution.py:60
  13.7 16.1 %scatter_custom_fusion.1 = s32[8192]{0:T(1024)} fusion(s32[4096]{0:T(1024)S(1)} %broadcast_select_fusion.2, s32[4096]{0:T(1024)S(1)} %get-tuple-element.186, s32[]{:T(128)} %constant.147.clone.1), kind=kCustom, calls=%fused_computation.109 | custom fusion | bytes 32772
  29.8 9.8 %all-to-all-start.1 = ((s32[1,32,256]{2,0,1:T(1,128)}), s32[1,32,256]{2,0,1:T(1,128)S(1)}, u32[]{:S(2)}, u32[]{:S(2)}) async-start(s32[1,32,256]{2,0,1:T(1,128)} %bitcast.8), calls=%async_computation.1 | async-start | bytes 65536 | tf_op jit(solution)/shard_map/all_to_all | solution.py:150
  41.4 12.8 %scatter_custom_fusion = f32[3,8192]{0,1:T(8,128)} fusion(s32[4096]{0:T(1024)S(1)} %bitcast.101, f32[4096,3]{1,0:T(8,128)S(1)} %copy.23, f32[]{:T(128)} %constant.145.clone.1), kind=kCustom, calls=%fused_computation.31 | custom fusion | bytes 98308 | tf_op jit(solution)/shard_map/scatter | solution.py:139
  54.2 3.5 %copy.24 = f32[3,32,256]{2,0,1:T(4,128)} copy(f32[3,32,256]{0,2,1:T(8,128)} %bitcast.82) | data formatting | bytes 196608 | tf_op jit(solution)/shard_map/reshape | solution.py:148
  57.9 9.8 %all-to-all-start = ((f32[3,32,256]{2,0,1:T(4,128)}), f32[3,32,256]{2,0,1:T(4,128)S(1)}, u32[]{:S(2)}, u32[]{:S(2)}) async-start(f32[3,32,256]{2,0,1:T(4,128)} %copy.24), calls=%async_computation | async-start | bytes 262144 | tf_op jit(solution)/shard_map/all_to_all | solution.py:147
  69.4 4.2 %all-to-all-done = f32[3,32,256]{2,0,1:T(4,128)S(1)} async-done(((f32[3,32,256]{2,0,1:T(4,128)}), f32[3,32,256]{2,0,1:T(4,128)S(1)}, u32[]{:S(2)}, u32[]{:S(2)}) %all-to-all-start) | async-done | bytes 98336 | tf_op jit(solution)/shard_map/all_to_all | solution.py:147
  74.2 30.3 %psum.22 = f32[2,4]{1,0:T(2,128)S(1)} all-reduce(f32[2,4]{1,0:T(2,128)S(1)} %pad_maximum_fusion.3), channel_id=1, replica_groups=mesh['ta'=32,'pb'=16] {'pb'}, use_global_device_ids=true, to_apply=%region_15.16 | all-reduce | flops 8 | bytes 64 | tf_op jit(solution)/shard_map/psum | solution.py:187
  104.6 8.0 %while.27 = (s32[]{:T(128)}, f32[384,96]{0,1:T(8,128)S(1)}, s32[4,2048]{1,0:T(4,128)S(1)}, s32[4,2048]{1,0:T(4,128)S(1)}, bf16[4,2048]{1,0:T(4,128)(2,1)S(1)}, /*index=5*/s32[]{:T(128)}, s32[]{:T(128)}) while((s32[]{:T(128)}, f32[384,96]{0,1:T(8,128)S(1)}, s32[4,2048]{1,0:T(4,128)S(1)}, s32[4,2048]{1,0:T(4,128)S(1)}, ...), condition=%wide.region_9.10_spmd.clone, body=%wide.region_8.9_spmd.clone.sunk | while | flops 153069568 | bytes 5517415 | solution.py:89
  105.6 1.0 convolution_add_fusion.3
  109.6 1.0 convolution_add_fusion.3
  113.7 2.5 collective-permute-start.2
  116.2 101.6 %all-reduce.6.cloned.1.call-done = f32[4,9216]{1,0:T(4,128)} async-done(((f32[4,9216]{1,0:T(4,128)}), f32[4,9216]{1,0:T(4,128)}) %all-reduce.6.cloned.1.call-update) | async-done | bytes 147472 | tf_op jit(solution)/shard_map/psum | solution.py:164
  217.9 1.0 fusion.37
  218.9 3.4 %collective-permute-start.1 = (f32[1,9216]{1,0:T(1,128)S(1)}, f32[1,9216]{1,0:T(1,128)S(1)}, u32[]{:S(2)}, u32[]{:S(2)}) collective-permute-start(f32[1,9216]{1,0:T(1,128)S(1)} %get-tuple-element.177), channel_id=1, source_target_pairs={{0,16},{16,32},{32,48},{48,64},{64,80},{80,96},{96,112},{112,128},... | collective-permute-start | bytes 110600 | tf_op jit(solution)/shard_map/ppermute | solution.py:24
  222.3 6.0 %collective-permute-start = (f32[1,9216]{1,0:T(1,128)S(1)}, f32[1,9216]{1,0:T(1,128)S(1)}, u32[]{:S(2)}, u32[]{:S(2)}) collective-permute-start(f32[1,9216]{1,0:T(1,128)S(1)} %get-tuple-element.176), channel_id=1, source_target_pairs={{16,0},{32,16},{48,32},{64,48},{80,64},{96,80},{112,96},{128,112},... | collective-permute-start | bytes 110600 | tf_op jit(solution)/shard_map/ppermute | solution.py:25
  228.5 1.2 collective-permute-done
  229.7 2.0 fusion.19
  231.8 45.5 %gather_fusion = f32[8192]{0:T(1024)S(1)} fusion(f32[36864]{0:T(1024)S(1)} %bitcast.81, s32[8192]{0:T(1024)S(1)} %broadcast_clamp_fusion), kind=kCustom, calls=%fused_computation | custom fusion | bytes 98304 | tf_op jit(solution)/shard_map/jit(_take)/gather | solution.py:168
  278.0 23.5 %psum.23 = f32[2,4]{1,0:T(2,128)S(1)} all-reduce(f32[2,4]{1,0:T(2,128)S(1)} %pad_maximum_fusion.4), channel_id=1, replica_groups=mesh['ta'=32,'pb'=16] {'pb'}, use_global_device_ids=true, to_apply=%region_20.21 | all-reduce | flops 8 | bytes 64 | tf_op jit(solution)/shard_map/psum | solution.py:187
  301.9 2.2 add_select_fusion.8
  304.3 1.9 collective-permute-start.3
  306.9 6.5 %collective-permute-done.3 = f32[2,1]{1,0:T(2,128)S(1)} collective-permute-done((f32[2,1]{1,0:T(2,128)S(1)}, f32[2,1]{1,0:T(2,128)S(1)}, u32[]{:S(2)}, u32[]{:S(2)}) %collective-permute-start.3) | collective-permute-done | bytes 40 | tf_op jit(solution)/shard_map/ppermute | solution.py:33
  (151 shorter events, 18.4 us)
Async XLA Ops:
  7.2 6.2 %copy-start.12 = (s32[2]{0:T(128)S(1)}, s32[2]{0:T(128)}, u32[]{:S(2)}) copy-start(s32[2]{0:T(128)} %constant.174) | copy-start | bytes 28
  7.2 6.3 %copy-start.11 = (s32[2]{0:T(128)S(1)}, s32[2]{0:T(128)}, u32[]{:S(2)}) copy-start(s32[2]{0:T(128)} %constant.171) | copy-start | bytes 28
  7.2 6.1 %copy-start = (s32[4096,1]{0,1:T(1,128)S(1)}, s32[4096,1]{0,1:T(1,128)}, u32[]{:S(2)}) copy-start(s32[4096,1]{0,1:T(1,128)} %param.18) | copy-start | bytes 49156
  7.2 6.4 %copy-start.4 = (s32[4096]{0:T(1024)S(1)}, s32[4096]{0:T(1024)}, u32[]{:S(2)}) copy-start(s32[4096]{0:T(1024)} %param.17) | copy-start | bytes 49156
  7.2 6.4 %copy-start.5 = (s32[4096]{0:T(1024)S(1)}, s32[4096]{0:T(1024)}, u32[]{:S(2)}) copy-start(s32[4096]{0:T(1024)} %param.19) | copy-start | bytes 49156
  7.2 32.4 %copy-start.6 = (bf16[4096]{0:T(1024)(128)(2,1)S(1)}, bf16[4096]{0:T(1024)(128)(2,1)}, u32[]{:S(2)}) copy-start(bf16[4096]{0:T(1024)(128)(2,1)} %param.16) | copy-start | bytes 24580
  7.2 32.4 %copy-start.7 = (f32[96]{0:T(128)S(1)}, f32[96]{0:T(128)}, u32[]{:S(2)}) copy-start(f32[96]{0:T(128)} %param.21) | copy-start | bytes 1156
  7.2 32.4 %copy-start.8 = (f32[96]{0:T(128)S(1)}, f32[96]{0:T(128)}, u32[]{:S(2)}) copy-start(f32[96]{0:T(128)} %param.20) | copy-start | bytes 1156
  7.3 33.0 %copy-start.3 = (f32[2,4096]{1,0:T(2,128)S(1)}, f32[2,4096]{1,0:T(2,128)}, u32[]{:S(2)}) copy-start(f32[2,4096]{1,0:T(2,128)} %param.15) | copy-start | bytes 98308
  29.8 28.1 %all-to-all-start.1 = ((s32[1,32,256]{2,0,1:T(1,128)}), s32[1,32,256]{2,0,1:T(1,128)S(1)}, u32[]{:S(2)}, u32[]{:S(2)}) async-start(s32[1,32,256]{2,0,1:T(1,128)} %bitcast.8), calls=%async_computation.1 | async-start | bytes 65536 | tf_op jit(solution)/shard_map/all_to_all | solution.py:150
  54.2 3.5 %copy-start.1 = (f32[96,96]{1,0:T(8,128)S(1)}, f32[96,96]{1,0:T(8,128)}, u32[]{:S(2)}) copy-start(f32[96,96]{1,0:T(8,128)} %param.25) | copy-start | bytes 110596
  54.2 3.6 %copy-start.2 = (f32[96,96]{1,0:T(8,128)S(1)}, f32[96,96]{1,0:T(8,128)}, u32[]{:S(2)}) copy-start(f32[96,96]{1,0:T(8,128)} %param.24) | copy-start | bytes 110596
  54.2 14.2 %copy-start.9 = (f32[96]{0:T(128)S(1)}, f32[96]{0:T(128)}, u32[]{:S(2)}) copy-start(f32[96]{0:T(128)} %param.23) | copy-start | bytes 1156
  54.2 14.2 %copy-start.10 = (f32[96]{0:T(128)S(1)}, f32[96]{0:T(128)}, u32[]{:S(2)}) copy-start(f32[96]{0:T(128)} %param.22) | copy-start | bytes 1156
  57.9 15.7 %all-to-all-start = ((f32[3,32,256]{2,0,1:T(4,128)}), f32[3,32,256]{2,0,1:T(4,128)S(1)}, u32[]{:S(2)}, u32[]{:S(2)}) async-start(f32[3,32,256]{2,0,1:T(4,128)} %copy.24), calls=%async_computation | async-start | bytes 262144 | tf_op jit(solution)/shard_map/all_to_all | solution.py:147
  67.7 150.2 %all-reduce.6.cloned.1.call-start = ((), (), s32[]{:S(2)}) async-start(), calls=%async_computation.2 | async-start | bytes 294912 | tf_op jit(solution)/shard_map/psum | solution.py:164
  113.7 187.8 %collective-permute-start.2 = (f32[2,1]{1,0:T(2,128)S(1)}, f32[2,1]{1,0:T(2,128)S(1)}, u32[]{:S(2)}, u32[]{:S(2)}) collective-permute-start(f32[2,1]{1,0:T(2,128)S(1)} %slice.85), channel_id=1, source_target_pairs={{0,16},{16,32},{32,48},{48,64},{64,80},{80,96},{96,112},{112,128},... | collective-permute-start | bytes 32 | tf_op jit(solution)/shard_map/ppermute | solution.py:33
  218.9 9.6 %collective-permute-start.1 = (f32[1,9216]{1,0:T(1,128)S(1)}, f32[1,9216]{1,0:T(1,128)S(1)}, u32[]{:S(2)}, u32[]{:S(2)}) collective-permute-start(f32[1,9216]{1,0:T(1,128)S(1)} %get-tuple-element.177), channel_id=1, source_target_pairs={{0,16},{16,32},{32,48},{48,64},{64,80},{80,96},{96,112},{112,128},... | collective-permute-start | bytes 110600 | tf_op jit(solution)/shard_map/ppermute | solution.py:24
  222.3 7.4 %collective-permute-start = (f32[1,9216]{1,0:T(1,128)S(1)}, f32[1,9216]{1,0:T(1,128)S(1)}, u32[]{:S(2)}, u32[]{:S(2)}) collective-permute-start(f32[1,9216]{1,0:T(1,128)S(1)} %get-tuple-element.176), channel_id=1, source_target_pairs={{16,0},{32,16},{48,32},{64,48},{80,64},{96,80},{112,96},{128,112},... | collective-permute-start | bytes 110600 | tf_op jit(solution)/shard_map/ppermute | solution.py:25
  304.3 9.1 %collective-permute-start.3 = (f32[2,1]{1,0:T(2,128)S(1)}, f32[2,1]{1,0:T(2,128)S(1)}, u32[]{:S(2)}, u32[]{:S(2)}) collective-permute-start(f32[2,1]{1,0:T(2,128)S(1)} %slice.89), channel_id=1, source_target_pairs={{0,16},{16,32},{32,48},{48,64},{64,80},{80,96},{96,112},{112,128},... | collective-permute-start | bytes 32 | tf_op jit(solution)/shard_map/ppermute | solution.py:33
Sparse Core Ops, SparseCore 0:
  113.8 104.0 all-reduce.5
where the time goes:
time: 321 us
  waiting for transfers between devices  114 us (36%)
  local copies, waits for them, and re-layouts  82.4 us (26%)
  blocking collectives  53.8 us (17%)
  starting transfers between devices  33.4 us (10%)
  other arithmetic  16.3 us (5%)
  between operations  14.6 us (5%)
  matrix products  6.37 us (2%)
    psum x1, waiting for transfers between devices, body(): summed = lax.psum(partial_value, 'pb')  102 us
    psum x2, blocking collectives, body(): bunching = lax.psum(local_sums, 'pb')  53.8 us
    gather x1, local copies, waits for them, and re-layouts, body(): kicked = got_float[1] + jnp.take(force_map.reshape(-1), combined)  45.5 us
    unnamed x30, local copies, waits for them, and re-layouts  16.7 us
    scatter x1, local copies, waits for them, and re-layouts, body(): send_float = jnp.zeros((3, slot_count), jnp.float32).at[:, position].set(...  12.8 us
    all_to_all x1, starting transfers between devices, body(): lax.all_to_all(send_index.reshape(1, groups, capacity), 'ta', split_axis=...  9.83 us
    all_to_all x1, starting transfers between devices, body(): lax.all_to_all(send_float.reshape(3, groups, capacity), 'ta', split_axis=...  9.79 us
    ppermute x2, waiting for transfers between devices, shifted(): lax.ppermute(value, axis, [(source, source + steps) for source in range(l...  6.48 us
  transfers between devices with their start and end apart: 7, of which 4 were waited for; matrix products, arithmetic and copies ran while one was open for 22% of the time, Pallas kernels for 0%

commit v1 on v0

--- a/solution.py
+++ b/solution.py
@@ -147,8 +147,16 @@
         lax.all_to_all(
             send_float.reshape(3, groups, capacity), "ta", split_axis=1, concat_axis=1, tiled=True
         ),
-        lax.all_to_all(
-            send_index.reshape(1, groups, capacity), "ta", split_axis=1, concat_axis=1, tiled=True
+        jnp.concatenate(
+            lax.all_to_all(
+                jnp.stack(
+                    jnp.split(send_index.reshape(1, groups, capacity), lax.axis_size("ta"), axis=1)
+                ),
+                "ta",
+                0,
+                0,
+            ),
+            axis=1,
         ),
     )
     got_float = got_float.reshape(3, slot_count)

time: 321 us -> 339 us (1.056)
  local copies, waits for them, and re-layouts: 82.4 us -> 99.9 us
    unnamed x30 -> x61, local copies, waits for them, and re-layouts: 16.7 us -> 33.6 us
  transfers between devices with their start and end apart: 7 -> 7, of which waited for: 4 -> 4; matrix products, arithmetic and copies ran while one was open for 22% -> 21% of each run, Pallas kernels for 0% -> 0%
where the time goes in v1:
time: 339 us; the launch traced here: 338 us
  waiting for transfers between devices  114 us (34%)
  local copies, waits for them, and re-layouts  99.9 us (29%)
  blocking collectives  53.8 us (16%)
  starting transfers between devices  33.4 us (10%)
  other arithmetic  16.3 us (5%)
  between operations  14.6 us (4%)
  matrix products  6.37 us (2%)
    psum x1, waiting for transfers between devices, body(): summed = lax.psum(partial_value, 'pb')  102 us
    psum x2, blocking collectives, body(): bunching = lax.psum(local_sums, 'pb')  53.8 us
    gather x1, local copies, waits for them, and re-layouts, body(): kicked = got_float[1] + jnp.take(force_map.reshape(-1), combined)  45.5 us
    unnamed x61, local copies, waits for them, and re-layouts  33.6 us
    scatter x1, local copies, waits for them, and re-layouts, body(): send_float = jnp.zeros((3, slot_count), jnp.float32).at[:, position].set(...  12.8 us
    all_to_all x1, starting transfers between devices, body(): lax.all_to_all(jnp.stack(jnp.split(send_index.reshape(1, groups, capacity...  9.83 us
    all_to_all x1, starting transfers between devices, body(): lax.all_to_all(send_float.reshape(3, groups, capacity), 'ta', split_axis=...  9.79 us
  transfers between devices with their start and end apart: 7, of which 4 were waited for; matrix products, arithmetic and copies ran while one was open for 21% of the time, Pallas kernels for 0%

profile of v1, /device:TPU:32, one launch (start us, length us, event | category | flops | bytes accessed | tf_op | source)
XLA Modules:
  0.0 338.4 jit_solution(14807000970858624350)
XLA Ops:
  7.8 1.4 reduce.17
  9.3 4.0 %while.26 = (s32[]{:T(128)}, f32[32]{0:T(128)S(1)}, f32[8,512]{1,0:T(8,128)S(1)}, bf16[8,512,32]{1,2,0:T(8,128)(2,1)S(1)}, s32[]{:T(128)}, /*index=5*/s32[]{:T(128)}) while((s32[]{:T(128)}, f32[32]{0:T(128)S(1)}, f32[8,512]{1,0:T(8,128)S(1)}, bf16[8,512,32]{1,2,0:T(8,128)(2,1)S(1)}, s32[]{:T(128)}, /*index=5*/s32[]{:T(128)}) %tuple.81), condition=%wide.region_3.4_spmd.clone, body=%wide.region_0.3_spmd.clone.sunk | while | flops 17399332 | bytes 106719 | solution.py:60
  13.7 15.5 %scatter_custom_fusion.1 = s32[8192]{0:T(1024)S(1)} fusion(s32[4096]{0:T(1024)S(1)} %broadcast_select_fusion.2, s32[4096]{0:T(1024)S(1)} %get-tuple-element.186, s32[]{:T(128)} %constant.147.clone.1), kind=kCustom, calls=%fused_computation.141 | custom fusion | bytes 32772
  47.3 9.8 %all-to-all-start.1 = ((s32[32,1,1,256]{3,2,1,0:T(1,128)}), s32[32,1,1,256]{3,2,1,0:T(1,128)S(1)}, u32[]{:S(2)}, u32[]{:S(2)}) async-start(s32[32,1,1,256]{3,2,1,0:T(1,128)} %constant_dynamic-update-slice_fusion), calls=%async_computation.1 | async-start | bytes 65536 | tf_op jit(solution)/shard_map/all_to_all | solution.py:151
  59.0 12.8 %scatter_custom_fusion = f32[3,8192]{0,1:T(8,128)} fusion(s32[4096]{0:T(1024)S(1)} %bitcast.228, f32[4096,3]{1,0:T(8,128)S(1)} %copy.23, f32[]{:T(128)} %constant.145.clone.1), kind=kCustom, calls=%fused_computation.31 | custom fusion | bytes 98308 | tf_op jit(solution)/shard_map/scatter | solution.py:139
  71.8 3.5 %copy.24 = f32[3,32,256]{2,0,1:T(4,128)} copy(f32[3,32,256]{0,2,1:T(8,128)} %bitcast.209) | data formatting | bytes 196608 | tf_op jit(solution)/shard_map/reshape | solution.py:148
  75.4 9.8 %all-to-all-start = ((f32[3,32,256]{2,0,1:T(4,128)}), f32[3,32,256]{2,0,1:T(4,128)S(1)}, u32[]{:S(2)}, u32[]{:S(2)}) async-start(f32[3,32,256]{2,0,1:T(4,128)} %copy.24), calls=%async_computation | async-start | bytes 262144 | tf_op jit(solution)/shard_map/all_to_all | solution.py:147
  87.0 4.2 %all-to-all-done = f32[3,32,256]{2,0,1:T(4,128)S(1)} async-done(((f32[3,32,256]{2,0,1:T(4,128)}), f32[3,32,256]{2,0,1:T(4,128)S(1)}, u32[]{:S(2)}, u32[]{:S(2)}) %all-to-all-start) | async-done | bytes 98336 | tf_op jit(solution)/shard_map/all_to_all | solution.py:147
  91.8 30.3 %psum.22 = f32[2,4]{1,0:T(2,128)S(1)} all-reduce(f32[2,4]{1,0:T(2,128)S(1)} %pad_maximum_fusion.3), channel_id=1, replica_groups=mesh['ta'=32,'pb'=16] {'pb'}, use_global_device_ids=true, to_apply=%region_15.16 | all-reduce | flops 8 | bytes 64 | tf_op jit(solution)/shard_map/psum | solution.py:195
  122.2 8.0 %while.27 = (s32[]{:T(128)}, f32[384,96]{0,1:T(8,128)S(1)}, s32[4,2048]{1,0:T(4,128)S(1)}, s32[4,2048]{1,0:T(4,128)S(1)}, bf16[4,2048]{1,0:T(4,128)(2,1)S(1)}, /*index=5*/s32[]{:T(128)}, s32[]{:T(128)}) while((s32[]{:T(128)}, f32[384,96]{0,1:T(8,128)S(1)}, s32[4,2048]{1,0:T(4,128)S(1)}, s32[4,2048]{1,0:T(4,128)S(1)}, ...), condition=%wide.region_9.10_spmd.clone, body=%wide.region_8.9_spmd.clone.sunk | while | flops 153069568 | bytes 5517415 | solution.py:89
  125.1 1.0 convolution_add_fusion.3
  129.2 1.0 convolution_add_fusion.3
  131.3 2.5 collective-permute-start.2
  133.8 101.6 %all-reduce.6.cloned.1.call-done = f32[4,9216]{1,0:T(4,128)} async-done(((f32[4,9216]{1,0:T(4,128)}), f32[4,9216]{1,0:T(4,128)}) %all-reduce.6.cloned.1.call-update) | async-done | bytes 147472 | tf_op jit(solution)/shard_map/psum | solution.py:172
  235.4 1.0 fusion.37
  236.5 3.4 collective-permute-start.1
  239.8 6.0 %collective-permute-start = (f32[1,9216]{1,0:T(1,128)S(1)}, f32[1,9216]{1,0:T(1,128)S(1)}, u32[]{:S(2)}, u32[]{:S(2)}) collective-permute-start(f32[1,9216]{1,0:T(1,128)S(1)} %get-tuple-element.176), channel_id=1, source_target_pairs={{16,0},{32,16},{48,32},{64,48},{80,64},{96,80},{112,96},{128,112},... | collective-permute-start | bytes 110600 | tf_op jit(solution)/shard_map/ppermute | solution.py:25
  246.1 1.2 collective-permute-done
  247.2 2.0 fusion.19
  249.3 45.5 %gather_fusion = f32[8192]{0:T(1024)S(1)} fusion(f32[36864]{0:T(1024)S(1)} %bitcast.208, s32[8192]{0:T(1024)S(1)} %broadcast_clamp_fusion), kind=kCustom, calls=%fused_computation | custom fusion | bytes 98304 | tf_op jit(solution)/shard_map/jit(_take)/gather | solution.py:176
  295.6 23.5 %psum.23 = f32[2,4]{1,0:T(2,128)S(1)} all-reduce(f32[2,4]{1,0:T(2,128)S(1)} %pad_maximum_fusion.4), channel_id=1, replica_groups=mesh['ta'=32,'pb'=16] {'pb'}, use_global_device_ids=true, to_apply=%region_20.21 | all-reduce | flops 8 | bytes 64 | tf_op jit(solution)/shard_map/psum | solution.py:195
  319.5 2.2 add_select_fusion.8
  321.8 1.9 collective-permute-start.3
  324.4 6.5 %collective-permute-done.3 = f32[2,1]{1,0:T(2,128)S(1)} collective-permute-done((f32[2,1]{1,0:T(2,128)S(1)}, f32[2,1]{1,0:T(2,128)S(1)}, u32[]{:S(2)}, u32[]{:S(2)}) %collective-permute-start.3) | collective-permute-done | bytes 40 | tf_op jit(solution)/shard_map/ppermute | solution.py:33
  (184 shorter events, 36.4 us)
Async XLA Ops:
  7.2 6.2 %copy-start.12 = (s32[2]{0:T(128)S(1)}, s32[2]{0:T(128)}, u32[]{:S(2)}) copy-start(s32[2]{0:T(128)} %constant.174) | copy-start | bytes 28
  7.2 6.3 %copy-start.11 = (s32[2]{0:T(128)S(1)}, s32[2]{0:T(128)}, u32[]{:S(2)}) copy-start(s32[2]{0:T(128)} %constant.171) | copy-start | bytes 28
  7.2 6.1 %copy-start = (s32[4096,1]{0,1:T(1,128)S(1)}, s32[4096,1]{0,1:T(1,128)}, u32[]{:S(2)}) copy-start(s32[4096,1]{0,1:T(1,128)} %param.18) | copy-start | bytes 49156
  7.2 6.4 %copy-start.4 = (s32[4096]{0:T(1024)S(1)}, s32[4096]{0:T(1024)}, u32[]{:S(2)}) copy-start(s32[4096]{0:T(1024)} %param.17) | copy-start | bytes 49156
  7.2 6.4 %copy-start.5 = (s32[4096]{0:T(1024)S(1)}, s32[4096]{0:T(1024)}, u32[]{:S(2)}) copy-start(s32[4096]{0:T(1024)} %param.19) | copy-start | bytes 49156
  7.2 49.9 %copy-start.6 = (bf16[4096]{0:T(1024)(128)(2,1)S(1)}, bf16[4096]{0:T(1024)(128)(2,1)}, u32[]{:S(2)}) copy-start(bf16[4096]{0:T(1024)(128)(2,1)} %param.16) | copy-start | bytes 24580
  7.2 49.9 %copy-start.7 = (f32[96]{0:T(128)S(1)}, f32[96]{0:T(128)}, u32[]{:S(2)}) copy-start(f32[96]{0:T(128)} %param.21) | copy-start | bytes 1156
  7.2 49.9 %copy-start.8 = (f32[96]{0:T(128)S(1)}, f32[96]{0:T(128)}, u32[]{:S(2)}) copy-start(f32[96]{0:T(128)} %param.20) | copy-start | bytes 1156
  7.3 50.5 %copy-start.3 = (f32[2,4096]{1,0:T(2,128)S(1)}, f32[2,4096]{1,0:T(2,128)}, u32[]{:S(2)}) copy-start(f32[2,4096]{1,0:T(2,128)} %param.15) | copy-start | bytes 98308
  47.3 28.1 %all-to-all-start.1 = ((s32[32,1,1,256]{3,2,1,0:T(1,128)}), s32[32,1,1,256]{3,2,1,0:T(1,128)S(1)}, u32[]{:S(2)}, u32[]{:S(2)}) async-start(s32[32,1,1,256]{3,2,1,0:T(1,128)} %constant_dynamic-update-slice_fusion), calls=%async_computation.1 | async-start | bytes 65536 | tf_op jit(solution)/shard_map/all_to_all | solution.py:151
  71.7 3.5 %copy-start.1 = (f32[96,96]{1,0:T(8,128)S(1)}, f32[96,96]{1,0:T(8,128)}, u32[]{:S(2)}) copy-start(f32[96,96]{1,0:T(8,128)} %param.25) | copy-start | bytes 110596
  71.7 3.6 %copy-start.2 = (f32[96,96]{1,0:T(8,128)S(1)}, f32[96,96]{1,0:T(8,128)}, u32[]{:S(2)}) copy-start(f32[96,96]{1,0:T(8,128)} %param.24) | copy-start | bytes 110596
  71.7 14.2 %copy-start.9 = (f32[96]{0:T(128)S(1)}, f32[96]{0:T(128)}, u32[]{:S(2)}) copy-start(f32[96]{0:T(128)} %param.23) | copy-start | bytes 1156
  71.7 14.2 %copy-start.10 = (f32[96]{0:T(128)S(1)}, f32[96]{0:T(128)}, u32[]{:S(2)}) copy-start(f32[96]{0:T(128)} %param.22) | copy-start | bytes 1156
  75.4 15.7 %all-to-all-start = ((f32[3,32,256]{2,0,1:T(4,128)}), f32[3,32,256]{2,0,1:T(4,128)S(1)}, u32[]{:S(2)}, u32[]{:S(2)}) async-start(f32[3,32,256]{2,0,1:T(4,128)} %copy.24), calls=%async_computation | async-start | bytes 262144 | tf_op jit(solution)/shard_map/all_to_all | solution.py:147
  85.2 150.2 %all-reduce.6.cloned.1.call-start = ((), (), s32[]{:S(2)}) async-start(), calls=%async_computation.2 | async-start | bytes 294912 | tf_op jit(solution)/shard_map/psum | solution.py:172
  131.3 187.8 %collective-permute-start.2 = (f32[2,1]{1,0:T(2,128)S(1)}, f32[2,1]{1,0:T(2,128)S(1)}, u32[]{:S(2)}, u32[]{:S(2)}) collective-permute-start(f32[2,1]{1,0:T(2,128)S(1)} %slice.85), channel_id=1, source_target_pairs={{0,16},{16,32},{32,48},{48,64},{64,80},{80,96},{96,112},{112,128},... | collective-permute-start | bytes 32 | tf_op jit(solution)/shard_map/ppermute | solution.py:33
  236.5 9.6 %collective-permute-start.1 = (f32[1,9216]{1,0:T(1,128)S(1)}, f32[1,9216]{1,0:T(1,128)S(1)}, u32[]{:S(2)}, u32[]{:S(2)}) collective-permute-start(f32[1,9216]{1,0:T(1,128)S(1)} %get-tuple-element.177), channel_id=1, source_target_pairs={{0,16},{16,32},{32,48},{48,64},{64,80},{80,96},{96,112},{112,128},... | collective-permute-start | bytes 110600 | tf_op jit(solution)/shard_map/ppermute | solution.py:24
  239.8 7.4 %collective-permute-start = (f32[1,9216]{1,0:T(1,128)S(1)}, f32[1,9216]{1,0:T(1,128)S(1)}, u32[]{:S(2)}, u32[]{:S(2)}) collective-permute-start(f32[1,9216]{1,0:T(1,128)S(1)} %get-tuple-element.176), channel_id=1, source_target_pairs={{16,0},{32,16},{48,32},{64,48},{80,64},{96,80},{112,96},{128,112},... | collective-permute-start | bytes 110600 | tf_op jit(solution)/shard_map/ppermute | solution.py:25
  321.8 9.1 %collective-permute-start.3 = (f32[2,1]{1,0:T(2,128)S(1)}, f32[2,1]{1,0:T(2,128)S(1)}, u32[]{:S(2)}, u32[]{:S(2)}) collective-permute-start(f32[2,1]{1,0:T(2,128)S(1)} %slice.89), channel_id=1, source_target_pairs={{0,16},{16,32},{32,48},{48,64},{64,80},{80,96},{96,112},{112,128},... | collective-permute-start | bytes 32 | tf_op jit(solution)/shard_map/ppermute | solution.py:33
Sparse Core Ops, SparseCore 0:
  131.3 104.0 all-reduce.5
